TPU v7x, 32 devices: a whole 2x2x4 slice. The times are simulated.
32 devices in a mesh: grp: 1, node: 8 (over z, y), dev: 4 (over x, core).
Axes of the slice: x: 2, y: 2, z: 4, core: 2. Of those that a mesh axis runs over, the one named last changes fastest.
Arguments:
- query_latent: bfloat16 [32, 128, 512], P(('grp', 'node', 'dev')), may hold values from -35 to 35
- query_rope: bfloat16 [32, 8192], P(('grp', 'node', 'dev')), may hold values from -5 to 5
- latent_cache: bfloat16 [32, 256, 512], P(('grp', 'node', 'dev')), may hold values from -5 to 5
- rope_cache: bfloat16 [32, 64, 256], P(('grp', 'node', 'dev')), may hold values from -5 to 5
- lengths: int32 [32], P(('grp', 'node', 'dev')), may hold values from 2 to 256, as said below
- moe_input: bfloat16 [32, 7168], P(('grp', 'node', 'dev')), may hold values from -6 to 6
- routes: int32 [32, 8], P(('grp', 'node', 'dev')), may hold values from 0 to 15, all different within a row; in each aligned block of 4 rows (0 to 3, 4 to 7, ...) at most 2 rows name the same one
- route_weight: bfloat16 [32, 8], P(('grp', 'node', 'dev')), may hold values from 0.029907227 to 0.29882812
- gate_weight: bfloat16 [32, 7168, 1024], P(('node', 'dev')), may hold values from -0.0625 to 0.0625
- up_weight: bfloat16 [32, 7168, 1024], P(('node', 'dev')), may hold values from -0.0625 to 0.0625
- down_weight: bfloat16 [32, 1024, 7168], P(('node', 'dev')), may hold values from -0.125 to 0.125
Outputs:
- attended: bfloat16 [32, 128, 512], P(('grp', 'node', 'dev'))
- moe_output: bfloat16 [32, 7168], P(('grp', 'node', 'dev'))
Inputs may be any that keep to these rules, and one draw needn't show every extreme that they name: `routes`: each row names 8 different experts; in each aligned block of 4 rows every expert is named by exactly 2 rows. `lengths`: every request has at least two live positions; in every draw some request has all 256.
All inputs are finite; a program needn't handle non-finite values.
Results may differ from a plain program's by a relative error of at most 0.0085.
Values may be sent and summed in bfloat16 or wider, within the bound.
No kernel may reach another device: no remote copies, remote signals or barrier semaphores. Data moves between devices by JAX's collectives and lax.ppermute only.
A program may use at most 128 MiB of HBM per device.

v0:
```python
import math
import jax
import jax.numpy as jnp
from jax import lax
from jax.sharding import PartitionSpec as P

E_NODE = 2
score_scale = 1.0 / math.sqrt(192.0)


def attention_scores(query_latent, rope_query, latent_block, rope_block):
    latent_part = jnp.einsum(
        "rhc,rtc->rht", query_latent, latent_block, preferred_element_type=jnp.float32
    )
    rope_part = jnp.einsum(
        "rhk,rkt->rht", rope_query, rope_block, preferred_element_type=jnp.float32
    )
    return score_scale * (latent_part + rope_part)


def normalize(scores, usable):
    masked = jnp.where(usable, scores, -jnp.inf)
    largest = jnp.max(masked, axis=-1, keepdims=True)
    powers = jnp.exp(masked - largest)
    return (powers / jnp.sum(powers, axis=-1, keepdims=True)).astype(jnp.bfloat16)


def attend(query_latent, query_rope, latent_cache, rope_cache, lengths):
    requests, head_count, latent = query_latent.shape
    context = latent_cache.shape[1]
    rope_query = query_rope.reshape(requests, head_count, -1)
    position = lax.broadcasted_iota(jnp.int32, (1, 1, context), 2)
    usable = position < lengths[:, None, None]
    block_width = min(128, context)
    blocks_live = (jnp.max(lengths) + block_width - 1) // block_width

    def score_block(counter, scores):
        block_start = counter * block_width
        latent_block = lax.dynamic_slice_in_dim(latent_cache, block_start, block_width, 1)
        rope_block = lax.dynamic_slice_in_dim(rope_cache, block_start, block_width, 2)
        block_scores = attention_scores(query_latent, rope_query, latent_block, rope_block)
        return lax.dynamic_update_slice_in_dim(scores, block_scores, block_start, 2)

    empty_scores = jnp.full((requests, head_count, context), -jnp.inf, jnp.float32)
    scores = lax.fori_loop(0, blocks_live, score_block, empty_scores)
    weights = normalize(scores, usable)

    def value_block(counter, accumulated):
        block_start = counter * block_width
        weight_block = lax.dynamic_slice_in_dim(weights, block_start, block_width, 2)
        latent_block = lax.dynamic_slice_in_dim(latent_cache, block_start, block_width, 1)
        return accumulated + jnp.einsum(
            "rht,rtc->rhc", weight_block, latent_block, preferred_element_type=jnp.float32
        )

    output = lax.fori_loop(
        0, blocks_live, value_block, jnp.zeros((requests, head_count, latent), jnp.float32)
    )
    return output.astype(jnp.bfloat16)


def shards(
    query_latent,
    query_rope,
    latent_cache,
    rope_cache,
    lengths,
    moe_input,
    routes,
    route_weight,
    gate_weight,
    up_weight,
    down_weight,
):
    attended = attend(query_latent, query_rope, latent_cache, rope_cache, lengths)
    feature_count = moe_input.shape[1]
    top = routes.shape[1]
    packed = jnp.concatenate(
        [moe_input, routes.astype(jnp.bfloat16), route_weight.astype(jnp.bfloat16)], axis=1
    )
    pool = lax.all_gather(packed, "dev", axis=0, tiled=True)
    pool_rows = pool[:, :feature_count]
    pool_routes = pool[:, feature_count : feature_count + top].astype(jnp.int32)
    pool_weights = pool[:, feature_count + top :]
    node_count = lax.axis_size("node")
    dev_count = lax.axis_size("dev")
    expert_half = lax.axis_index("dev") // (dev_count // E_NODE)
    pooled = pool_rows.shape[0]
    slot_count = pooled * pool_routes.shape[1] // (E_NODE * node_count)
    targets = jnp.arange(node_count, dtype=jnp.int32) * E_NODE + expert_half
    matches = pool_routes[:, :, None] == targets[None, None, :]
    chosen = jnp.sum(matches.astype(jnp.int32), axis=1)
    route_share = jnp.sum(
        jnp.where(matches, pool_weights[:, :, None].astype(jnp.float32), 0.0), axis=1
    )
    before = jnp.cumsum(chosen, axis=0) - chosen
    copies = 1
    per_copy = slot_count // copies
    slot_index = jnp.arange(slot_count, dtype=jnp.int32).reshape(1, copies, per_copy, 1)
    selection = (chosen.T[:, None, None, :] == 1) & (before.T[:, None, None, :] == slot_index)
    selector = selection.astype(jnp.bfloat16)
    weighted = (selection.astype(jnp.float32) * route_share.T[:, None, None, :]).astype(
        jnp.bfloat16
    )
    outgoing = jnp.einsum("ncsp,pd->cnsd", selector, pool_rows, preferred_element_type=jnp.float32)
    outgoing = outgoing.astype(jnp.bfloat16).reshape(copies * node_count, per_copy, feature_count)
    weighted, outgoing = (weighted, outgoing)
    arrived = lax.all_to_all(outgoing, "node", split_axis=0, concat_axis=0, tiled=True)
    peer_count, slot_total, width_total = arrived.shape
    flattened = arrived.reshape(peer_count * slot_total, width_total)
    gate_sum = jnp.dot(flattened, gate_weight[0], preferred_element_type=jnp.float32)
    up_sum = jnp.dot(flattened, up_weight[0], preferred_element_type=jnp.float32)
    hidden = (jax.nn.silu(gate_sum) * up_sum).astype(jnp.bfloat16)
    produced = jnp.dot(hidden, down_weight[0], preferred_element_type=jnp.float32).astype(
        jnp.bfloat16
    )
    partial_value = produced.reshape(peer_count, slot_total, width_total)
    returned = lax.all_to_all(partial_value, "node", split_axis=0, concat_axis=0, tiled=True)
    returned = returned.reshape(copies, node_count, slot_count // copies, feature_count)
    pool_sum = jnp.einsum("ncsp,cnsd->pd", weighted, returned, preferred_element_type=jnp.float32)
    if dev_count > 8:
        combined = lax.psum_scatter(pool_sum, "dev", scatter_dimension=0, tiled=True)
        return (attended, combined.astype(jnp.bfloat16))
    own = lax.axis_index("dev")
    rows_per = pooled // dev_count
    combined = lax.dynamic_slice_in_dim(pool_sum, own * rows_per, rows_per, 0)
    for shift in range(1, dev_count):
        target = (own + shift) % dev_count
        outgoing_part = lax.dynamic_slice_in_dim(pool_sum, target * rows_per, rows_per, 0)
        combined = combined + lax.ppermute(
            outgoing_part, "dev", [(i, (i + shift) % dev_count) for i in range(dev_count)]
        )
    return (attended, combined.astype(jnp.bfloat16))


def solution(mesh):
    in_specs = (
        P(("grp", "node", "dev"), None, None),
        P(("grp", "node", "dev"), None),
        P(("grp", "node", "dev"), None, None),
        P(("grp", "node", "dev"), None, None),
        P(("grp", "node", "dev")),
        P(("grp", "node", "dev"), None),
        P(("grp", "node", "dev"), None),
        P(("grp", "node", "dev"), None),
        P(("node", "dev"), None, None),
        P(("node", "dev"), None, None),
        P(("node", "dev"), None, None),
    )
    out_specs = (P(("grp", "node", "dev"), None, None), P(("grp", "node", "dev"), None))
    return jax.shard_map(shards, mesh=mesh, in_specs=in_specs, out_specs=out_specs, check_vma=False)
```

profile of v0, /device:TPU:0, one launch (start us, length us, event | category | flops | bytes accessed | tf_op | source)
XLA Modules:
  0.0 65.0 jit_solution(8729867085943102680)
XLA Ops:
  0.7 0.7 %convert_element_type.47 = bf16[1,8]{1,0:T(2,128)(2,1)S(1)} convert(s32[1,8]{1,0:T(1,128)} %param.21) | non-fusion elementwise | flops 8 | bytes 48 | tf_op jit(solution)/shard_map/convert_element_type | solution.py:79
  1.3 0.9 %concatenate.3 = bf16[1,7184]{1,0:T(2,128)(2,1)S(1)} concatenate(bf16[1,7168]{1,0:T(2,128)(2,1)} %param.20, bf16[1,8]{1,0:T(2,128)(2,1)S(1)} %convert_element_type.47, bf16[1,8]{1,0:T(2,128)(2,1)} %param.22), dimensions={1} | concatenate | bytes 28736 | tf_op jit(solution)/shard_map/concatenate | solution.py:78
  2.2 6.4 %all-gather = bf16[4,1,7184]{2,1,0:T(2,128)(2,1)S(1)} all-gather(bf16[1,1,7184]{2,1,0:T(2,128)(2,1)S(1)} %bitcast.86), channel_id=1, replica_groups=mesh['grp'=1,'node'=8,'dev'=4] {'dev'}, dimensions={0}, use_global_device_ids=true | all-gather | bytes 71840 | tf_op jit(solution)/shard_map/all_gather | solution.py:81
  8.6 0.1 slice_convert_fusion
  8.7 0.1 fusion.43
  8.8 0.3 fusion.26
  9.1 0.9 %copy.30 = bf16[8,2,7168]{2,1,0:T(2,128)(2,1)} copy(bf16[8,2,7168]{2,0,1:T(8,128)(2,1)S(1)} %fusion.26) | data formatting | bytes 458752 | tf_op jit(solution)/shard_map/reshape | solution.py:106
  10.0 6.3 %all-to-all-start = ((bf16[8,2,7168]{2,1,0:T(2,128)(2,1)}), bf16[8,2,7168]{2,1,0:T(2,128)(2,1)S(1)}, u32[]{:S(2)}, u32[]{:S(2)}) async-start(bf16[8,2,7168]{2,1,0:T(2,128)(2,1)} %copy.30), calls=%async_computation | async-start | bytes 458752 | tf_op jit(solution)/shard_map/all_to_all | solution.py:108
  16.9 0.8 %reduce.2 = bf16[8192]{0:T(1024)(128)(2,1)S(1)} reduce(bf16[1,8192]{1,0:T(2,128)(2,1)} %param.16, bf16[]{:T(256)} %constant.100), dimensions={0}, to_apply=%param.16.reduce_sub_computation | reduce | bytes 32770 | tf_op args[1]
  17.8 0.1 reshape.91
  17.9 2.2 %while.20 = (s32[]{:T(128)}, f32[1,128,256]{2,1,0:T(8,128)S(1)}, s32[]{:T(128)}, bf16[1,256,512]{2,1,0:T(8,128)(2,1)}, bf16[1,128,512]{2,1,0:T(8,128)(2,1)}, /*i...) while((s32[]{:T(128)}, f32[1,128,256]{2,1,0:T(8,128)S(1)}, ...), condition=%wide.region_1.2_spmd, body=%wide.region_0.0_spmd.sunk | while | flops 18907140 | bytes 753831 | solution.py:45
  17.9 1.2 %fusion.70 = f32[128,128]{1,0:T(8,128)S(1)} fusion(bf16[1,128,512]{2,1,0:T(8,128)(2,1)} %get-tuple-element.236, bf16[1,256,512]{2,1,0:T(8,128)(2,1)} %get-tuple-element.235, s32[]{:T(128)S(6)} %select_n.73), kind=kOutput, calls=%fused_computation.3.clone.1 | convolution fusion | flops 16777216 | bytes 327684 | tf_op jit(solution)/shard_map/while/body/rhc,rtc->rht/dot_general | solution.py:12
  19.1 0.9 %fusion.71 = f32[1,128,128]{1,2,0:T(8,128)S(1)} fusion(f32[128,128]{1,0:T(8,128)S(1)} %fusion.70, bf16[1,128,64]{2,1,0:T(8,128)(2,1)S(1)} %get-tuple-element.238, bf16[1,64,256]{2,1,0:T(8,128)(2,1)} %get-tuple-element.237, s32[]{:T(128)S(6)} %select_n.73), kind=kOutput, calls=%fused_computation.2.clone.1 | convolution fusion | flops 2129920 | bytes 163844 | tf_op jit(solution)/shard_map/while/body/rhk,rkt->rht/dot_general | solution.py:15
  20.0 0.1 copy.41
  20.1 0.1 select_reduce_fusion
  20.2 5.0 %all-to-all-done = bf16[8,2,7168]{2,1,0:T(2,128)(2,1)S(1)} async-done(((bf16[8,2,7168]{2,1,0:T(2,128)(2,1)}), bf16[8,2,7168]{2,1,0:T(2,128)(2,1)S(1)}, u32[]{:S(2)}, u32[]{:S(2)}) %all-to-all-start) | async-done | bytes 229408 | tf_op jit(solution)/shard_map/all_to_all | solution.py:108
  25.2 0.1 reshape.93
  25.3 7.2 %fusion.21 = f32[16,1024]{1,0:T(8,128)S(1)} fusion(bf16[16,7168]{1,0:T(8,128)(2,1)S(1)} %reshape.93, bf16[1,7168,1024]{2,1,0:T(8,128)(2,1)} %param.23), kind=kOutput, calls=%fused_computation.24 | convolution fusion | flops 234881024 | bytes 14974976 | tf_op jit(solution)/shard_map/dot_general | solution.py:111
  32.5 0.0 copy-start
  32.5 13.3 %fusion.23 = bf16[16,7168]{1,0:T(8,128)(2,1)S(1)} fusion(bf16[1,1024,7168]{2,1,0:T(8,128)(2,1)} %param.25, bf16[16,7168]{1,0:T(8,128)(2,1)S(1)} %reshape.93, bf16[1,7168,1024]{2,1,0:T(8,128)(2,1)} %param.24, f32[16,1024]{1,0:T(8,128)S(1)} %fusion.21), kind=kOutput, calls=%fused_computation.27 | convolution fusion | flops 469975040 | bytes 29884416 | tf_op jit(solution)/shard_map/dot_general | solution.py:114
  45.8 0.8 %reshape.94 = bf16[8,2,7168]{2,1,0:T(2,128)(2,1)} reshape(bf16[16,7168]{1,0:T(8,128)(2,1)S(1)} %fusion.23) | data formatting | bytes 458752 | tf_op jit(solution)/shard_map/reshape | solution.py:117
  46.6 3.4 %all-to-all-start.1 = ((bf16[8,2,7168]{2,1,0:T(2,128)(2,1)}), bf16[8,2,7168]{2,1,0:T(2,128)(2,1)S(1)}, u32[]{:S(2)}, u32[]{:S(2)}) async-start(bf16[8,2,7168]{2,1,0:T(2,128)(2,1)} %reshape.94), calls=%async_computation.1 | async-start | bytes 458752 | tf_op jit(solution)/shard_map/all_to_all | solution.py:118
  50.0 0.1 fusion.44
  50.1 0.2 fusion.36
  50.3 0.1 divide_convert_fusion
  50.4 7.9 %all-to-all-done.1 = bf16[8,2,7168]{2,1,0:T(2,128)(2,1)S(1)} async-done(((bf16[8,2,7168]{2,1,0:T(2,128)(2,1)}), bf16[8,2,7168]{2,1,0:T(2,128)(2,1)S(1)}, u32[]{:S(2)}, u32[]{:S(2)}) %all-to-all-start.1) | async-done | bytes 229408 | tf_op jit(solution)/shard_map/all_to_all | solution.py:118
  58.4 0.2 convolution_bitcast_fusion.1
  58.6 0.1 constant_dynamic-slice_fusion.2
  58.7 0.1 collective-permute-start
  58.7 1.7 %collective-permute-start.2 = (f32[1,7168]{1,0:T(1,128)S(1)}, f32[1,7168]{1,0:T(1,128)S(1)}, u32[]{:S(2)}, u32[]{:S(2)}) collective-permute-start(f32[1,7168]{1,0:T(1,128)S(1)} %get-tuple-element.130), channel_id=1, source_target_pairs={{0,3},{1,0},{2,1},{3,2},{4,7},{5,4},{6,5},{7,6},{8,11},{9,8},{10,9... | collective-permute-start | bytes 86024 | tf_op jit(solution)/shard_map/ppermute | solution.py:130
  60.5 1.5 %collective-permute-start.1 = (f32[1,7168]{1,0:T(1,128)S(1)}, f32[1,7168]{1,0:T(1,128)S(1)}, u32[]{:S(2)}, u32[]{:S(2)}) collective-permute-start(f32[1,7168]{1,0:T(1,128)S(1)} %get-tuple-element.131), channel_id=1, source_target_pairs={{0,2},{1,3},{2,0},{3,1},{4,6},{5,7},{6,4},{7,5},{8,10},{9,11},{10,... | collective-permute-start | bytes 86024 | tf_op jit(solution)/shard_map/ppermute | solution.py:130
  62.0 0.0 copy-done
  62.0 0.2 while.21
  62.0 0.2 fusion.74
  62.2 0.7 %convert_element_type.46 = bf16[1,128,512]{2,1,0:T(8,128)(2,1)} convert(f32[1,128,512]{2,1,0:T(8,128)S(1)} %get-tuple-element.69) | non-fusion elementwise | flops 65536 | bytes 393216 | tf_op jit(solution)/shard_map/convert_element_type | solution.py:59
  62.9 0.0 collective-permute-done
  62.9 0.0 collective-permute-done.2
  62.9 1.4 %collective-permute-done.1 = f32[1,7168]{1,0:T(1,128)S(1)} collective-permute-done((f32[1,7168]{1,0:T(1,128)S(1)}, f32[1,7168]{1,0:T(1,128)S(1)}, u32[]{:S(2)}, u32[]{:S(2)}) %collective-permute-start.1) | collective-permute-done | bytes 28704 | tf_op jit(solution)/shard_map/ppermute | solution.py:130
  64.4 0.7 %add_convert_fusion = bf16[1,7168]{1,0:T(2,128)(2,1)} fusion(f32[1,7168]{1,0:T(1,128)S(1)} %collective-permute-done.2, f32[1,7168]{1,0:T(1,128)S(1)} %collective-permute-done.1, f32[1,7168]{1,0:T(1,128)S(1)} %collective-permute-done, f32[4,7168]{1,0:T(4,128)S(1)} %convolution_bitcast_fusion.1, s32[]{:T(128)S(6)} %select_n.55), kind=kLoop, calls=%fused_computation.45 | loop fusion | flops 28672 | bytes 129028 | tf_op jit(solution)/shard_map/convert_element_type | solution.py:133
  (9 shorter events, 0.1 us)
Async XLA Ops:
  10.0 15.2 %all-to-all-start = ((bf16[8,2,7168]{2,1,0:T(2,128)(2,1)}), bf16[8,2,7168]{2,1,0:T(2,128)(2,1)S(1)}, u32[]{:S(2)}, u32[]{:S(2)}) async-start(bf16[8,2,7168]{2,1,0:T(2,128)(2,1)} %copy.30), calls=%async_computation | async-start | bytes 458752 | tf_op jit(solution)/shard_map/all_to_all | solution.py:108
  32.5 29.5 %copy-start = (bf16[1,256,512]{2,1,0:T(8,128)(2,1)S(1)}, bf16[1,256,512]{2,1,0:T(8,128)(2,1)}, u32[]{:S(2)}) copy-start(bf16[1,256,512]{2,1,0:T(8,128)(2,1)} %get-tuple-element.270) | copy-start | bytes 786436
  46.6 11.8 %all-to-all-start.1 = ((bf16[8,2,7168]{2,1,0:T(2,128)(2,1)}), bf16[8,2,7168]{2,1,0:T(2,128)(2,1)S(1)}, u32[]{:S(2)}, u32[]{:S(2)}) async-start(bf16[8,2,7168]{2,1,0:T(2,128)(2,1)} %reshape.94), calls=%async_computation.1 | async-start | bytes 458752 | tf_op jit(solution)/shard_map/all_to_all | solution.py:118
  58.7 4.2 %collective-permute-start = (f32[1,7168]{1,0:T(1,128)S(1)}, f32[1,7168]{1,0:T(1,128)S(1)}, u32[]{:S(2)}, u32[]{:S(2)}) collective-permute-start(f32[1,7168]{1,0:T(1,128)S(1)} %get-tuple-element.129), channel_id=1, source_target_pairs={{0,1},{1,2},{2,3},{3,0},{4,5},{5,6},{6,7},{7,4},{8,9},{9,10},{10,1... | collective-permute-start | bytes 86024 | tf_op jit(solution)/shard_map/ppermute | solution.py:130
  58.7 4.2 %collective-permute-start.2 = (f32[1,7168]{1,0:T(1,128)S(1)}, f32[1,7168]{1,0:T(1,128)S(1)}, u32[]{:S(2)}, u32[]{:S(2)}) collective-permute-start(f32[1,7168]{1,0:T(1,128)S(1)} %get-tuple-element.130), channel_id=1, source_target_pairs={{0,3},{1,0},{2,1},{3,2},{4,7},{5,4},{6,5},{7,6},{8,11},{9,8},{10,9... | collective-permute-start | bytes 86024 | tf_op jit(solution)/shard_map/ppermute | solution.py:130
  60.5 3.9 %collective-permute-start.1 = (f32[1,7168]{1,0:T(1,128)S(1)}, f32[1,7168]{1,0:T(1,128)S(1)}, u32[]{:S(2)}, u32[]{:S(2)}) collective-permute-start(f32[1,7168]{1,0:T(1,128)S(1)} %get-tuple-element.131), channel_id=1, source_target_pairs={{0,2},{1,3},{2,0},{3,1},{4,6},{5,7},{6,4},{7,5},{8,10},{9,11},{10,... | collective-permute-start | bytes 86024 | tf_op jit(solution)/shard_map/ppermute | solution.py:130
where the time goes:
time: 65.6 us; the launch traced here: 65 us
  matrix products  23.2 us (35%)
  waiting for transfers between devices  14.3 us (22%)
  starting transfers between devices  12.9 us (20%)
  blocking collectives  6.39 us (10%)
  other arithmetic  3.57 us (5%)
  local copies, waits for them, and re-layouts  2.96 us (5%)
  between operations  1.47 us (2%)
    dot_general x1, matrix products, shards(): jnp.dot(hidden, down_weight[0], preferred_element_type=jnp.float32)  13.3 us
    all_to_all x1, waiting for transfers between devices, shards(): lax.all_to_all(partial_value, 'node', split_axis=0, concat_axis=0, tiled=...  7.94 us
    dot_general x1, matrix products, shards(): jnp.dot(flattened, gate_weight[0], preferred_element_type=jnp.float32)  7.17 us
    all_gather x1, blocking collectives, shards(): pool = lax.all_gather(packed, 'dev', axis=0, tiled=True)  6.39 us
    all_to_all x1, starting transfers between devices, shards(): lax.all_to_all(outgoing, 'node', split_axis=0, concat_axis=0, tiled=True)  6.26 us
    all_to_all x1, waiting for transfers between devices, shards(): lax.all_to_all(outgoing, 'node', split_axis=0, concat_axis=0, tiled=True)  4.97 us
    all_to_all x1, starting transfers between devices, shards(): lax.all_to_all(partial_value, 'node', split_axis=0, concat_axis=0, tiled=...  3.4 us
    ppermute x3, starting transfers between devices, shards(): lax.ppermute(outgoing_part, 'dev', [(i, (i + shift) % dev_count) for i in...  3.28 us
  transfers between devices with their start and end apart: 5, of which 3 were waited for; matrix products, arithmetic and copies ran while one was open for 7% of the time, Pallas kernels for 0%

commit v1 on v0

--- a/solution.py
+++ b/solution.py
@@ -78,7 +78,12 @@
     packed = jnp.concatenate(
         [moe_input, routes.astype(jnp.bfloat16), route_weight.astype(jnp.bfloat16)], axis=1
     )
-    pool = lax.all_gather(packed, "dev", axis=0, tiled=True)
+    ring = [packed]
+    for hop in range(3):
+        ring.append(lax.ppermute(ring[-1], "dev", [(dev, (dev + 1) % 4) for dev in range(4)]))
+    pool = jnp.roll(
+        jnp.concatenate(ring[::-1], axis=0), (lax.axis_index("dev") + 1) * ring[0].shape[0], axis=0
+    )
     pool_rows = pool[:, :feature_count]
     pool_routes = pool[:, feature_count : feature_count + top].astype(jnp.int32)
     pool_weights = pool[:, feature_count + top :]

time: 65.6 us -> 69.8 us (1.064)
  waiting for transfers between devices: 14.3 us -> 24.2 us
  blocking collectives: 6.39 us -> 0 us
    ppermute x0 -> x3, waiting for transfers between devices: none -> 8.26 us  [shards(): lax.ppermute(ring[-1], 'dev', [(dev, (dev + 1) % 4) for dev in range(4)])]
    all_gather x1 -> x0, blocking collectives: 6.39 us -> none  [shards(): pool = lax.all_gather(packed, 'dev', axis=0, tiled=True)]
    all_to_all x1, waiting for transfers between devices: 4.97 us -> 6.17 us  [shards(): lax.all_to_all(outgoing, 'node', split_axis=0, concat_axis=0, tiled=True)]
  transfers between devices with their start and end apart: 5 -> 8, of which waited for: 3 -> 6; matrix products, arithmetic and copies ran while one was open for 7% -> 6% of each run, Pallas kernels for 0% -> 0%
where the time goes in v1:
time: 69.8 us; the launch traced here: 69.2 us
  waiting for transfers between devices  24.2 us (35%)
  matrix products  23.2 us (33%)
  starting transfers between devices  13.3 us (19%)
  other arithmetic  3.58 us (5%)
  local copies, waits for them, and re-layouts  3.28 us (5%)
  between operations  1.46 us (2%)
    dot_general x1, matrix products, shards(): jnp.dot(hidden, down_weight[0], preferred_element_type=jnp.float32)  13.3 us
    ppermute x3, waiting for transfers between devices, shards(): lax.ppermute(ring[-1], 'dev', [(dev, (dev + 1) % 4) for dev in range(4)])  8.26 us
    all_to_all x1, waiting for transfers between devices, shards(): lax.all_to_all(partial_value, 'node', split_axis=0, concat_axis=0, tiled=...  7.66 us
    dot_general x1, matrix products, shards(): jnp.dot(flattened, gate_weight[0], preferred_element_type=jnp.float32)  7.17 us
    all_to_all x1, starting transfers between devices, shards(): lax.all_to_all(outgoing, 'node', split_axis=0, concat_axis=0, tiled=True)  6.64 us
    all_to_all x1, waiting for transfers between devices, shards(): lax.all_to_all(outgoing, 'node', split_axis=0, concat_axis=0, tiled=True)  6.17 us
    all_to_all x1, starting transfers between devices, shards(): lax.all_to_all(partial_value, 'node', split_axis=0, concat_axis=0, tiled=...  3.4 us
    ppermute x3, starting transfers between devices, shards(): lax.ppermute(outgoing_part, 'dev', [(i, (i + shift) % dev_count) for i in...  2.6 us
  transfers between devices with their start and end apart: 8, of which 6 were waited for; matrix products, arithmetic and copies ran while one was open for 6% of the time, Pallas kernels for 0%

profile of v1, /device:TPU:0, one launch (start us, length us, event | category | flops | bytes accessed | tf_op | source)
XLA Modules:
  0.0 69.2 jit_solution(14331962154739163052)
XLA Ops:
  0.6 0.7 convert_element_type.47
  1.3 0.9 %concatenate.9 = bf16[1,7184]{1,0:T(2,128)(2,1)S(1)} concatenate(bf16[1,7168]{1,0:T(2,128)(2,1)} %param.20, bf16[1,8]{1,0:T(2,128)(2,1)S(1)} %convert_element_type.47, bf16[1,8]{1,0:T(2,128)(2,1)} %param.22), dimensions={1} | concatenate | bytes 28736 | tf_op jit(solution)/shard_map/concatenate | solution.py:78
  2.2 0.5 collective-permute-start
  2.6 3.5 %collective-permute-done = bf16[1,7184]{1,0:T(2,128)(2,1)S(1)} collective-permute-done((bf16[1,7184]{1,0:T(2,128)(2,1)S(1)}, bf16[1,7184]{1,0:T(2,128)(2,1)S(1)}, u32[]{:S(2)}, u32[]{:S(2)}) %collective-permute-start) | collective-permute-done | bytes 14400 | tf_op jit(solution)/shard_map/ppermute | solution.py:83
  6.1 0.1 collective-permute-start.1
  6.2 3.2 %collective-permute-done.1 = bf16[1,7184]{1,0:T(2,128)(2,1)S(1)} collective-permute-done((bf16[1,7184]{1,0:T(2,128)(2,1)S(1)}, bf16[1,7184]{1,0:T(2,128)(2,1)S(1)}, u32[]{:S(2)}, u32[]{:S(2)}) %collective-permute-start.1) | collective-permute-done | bytes 14400 | tf_op jit(solution)/shard_map/ppermute | solution.py:83
  9.4 0.1 collective-permute-start.2
  10.2 0.8 %reduce.2 = bf16[8192]{0:T(1024)(128)(2,1)S(1)} reduce(bf16[1,8192]{1,0:T(2,128)(2,1)} %param.16, bf16[]{:T(256)} %constant.114), dimensions={0}, to_apply=%param.16.reduce_sub_computation | reduce | bytes 32770 | tf_op args[1]
  11.0 0.1 reshape.91
  11.1 1.6 %collective-permute-done.2 = bf16[1,7184]{1,0:T(2,128)(2,1)S(1)} collective-permute-done((bf16[1,7184]{1,0:T(2,128)(2,1)S(1)}, bf16[1,7184]{1,0:T(2,128)(2,1)S(1)}, u32[]{:S(2)}, u32[]{:S(2)}) %collective-permute-start.2) | collective-permute-done | bytes 14400 | tf_op jit(solution)/shard_map/ppermute | solution.py:83
  12.7 0.3 concatenate.10
  13.0 0.1 dynamic-slice_convert_fusion
  13.1 0.1 fusion.43
  13.3 0.3 fusion.26
  13.5 0.9 %copy.26 = bf16[8,2,7168]{2,1,0:T(2,128)(2,1)} copy(bf16[8,2,7168]{2,0,1:T(8,128)(2,1)S(1)} %fusion.26) | data formatting | bytes 458752 | tf_op jit(solution)/shard_map/reshape | solution.py:111
  14.5 6.6 %all-to-all-start = ((bf16[8,2,7168]{2,1,0:T(2,128)(2,1)}), bf16[8,2,7168]{2,1,0:T(2,128)(2,1)S(1)}, u32[]{:S(2)}, u32[]{:S(2)}) async-start(bf16[8,2,7168]{2,1,0:T(2,128)(2,1)} %copy.26), calls=%async_computation | async-start | bytes 458752 | tf_op jit(solution)/shard_map/all_to_all | solution.py:113
  21.1 2.2 %while.20 = (s32[]{:T(128)}, f32[1,128,256]{2,1,0:T(8,128)S(1)}, s32[]{:T(128)}, bf16[1,256,512]{2,1,0:T(8,128)(2,1)}, bf16[1,128,512]{2,1,0:T(8,128)(2,1)}, /*i...) while((s32[]{:T(128)}, f32[1,128,256]{2,1,0:T(8,128)S(1)}, ...), condition=%wide.region_1.2_spmd, body=%wide.region_0.0_spmd.sunk | while | flops 18907140 | bytes 753831 | solution.py:45
  21.1 1.2 %fusion.71 = f32[128,128]{1,0:T(8,128)S(1)} fusion(bf16[1,128,512]{2,1,0:T(8,128)(2,1)} %get-tuple-element.229, bf16[1,256,512]{2,1,0:T(8,128)(2,1)} %get-tuple-element.228, s32[]{:T(128)S(6)} %select_n.84), kind=kOutput, calls=%fused_computation.3.clone.1 | convolution fusion | flops 16777216 | bytes 327684 | tf_op jit(solution)/shard_map/while/body/rhc,rtc->rht/dot_general | solution.py:12
  22.3 0.9 %fusion.72 = f32[1,128,128]{1,2,0:T(8,128)S(1)} fusion(f32[128,128]{1,0:T(8,128)S(1)} %fusion.71, bf16[1,128,64]{2,1,0:T(8,128)(2,1)S(1)} %get-tuple-element.231, bf16[1,64,256]{2,1,0:T(8,128)(2,1)} %get-tuple-element.230, s32[]{:T(128)S(6)} %select_n.84), kind=kOutput, calls=%fused_computation.2.clone.1 | convolution fusion | flops 2129920 | bytes 163844 | tf_op jit(solution)/shard_map/while/body/rhk,rkt->rht/dot_general | solution.py:15
  23.2 0.1 copy.34
  23.4 0.1 select_reduce_fusion
  23.5 6.2 %all-to-all-done = bf16[8,2,7168]{2,1,0:T(2,128)(2,1)S(1)} async-done(((bf16[8,2,7168]{2,1,0:T(2,128)(2,1)}), bf16[8,2,7168]{2,1,0:T(2,128)(2,1)S(1)}, u32[]{:S(2)}, u32[]{:S(2)}) %all-to-all-start) | async-done | bytes 229408 | tf_op jit(solution)/shard_map/all_to_all | solution.py:113
  29.6 0.1 reshape.93
  29.7 7.2 %fusion.21 = f32[16,1024]{1,0:T(8,128)S(1)} fusion(bf16[16,7168]{1,0:T(8,128)(2,1)S(1)} %reshape.93, bf16[1,7168,1024]{2,1,0:T(8,128)(2,1)} %param.23), kind=kOutput, calls=%fused_computation.24 | convolution fusion | flops 234881024 | bytes 14974976 | tf_op jit(solution)/shard_map/dot_general | solution.py:116
  36.9 0.0 copy-start
  36.9 13.3 %fusion.23 = bf16[16,7168]{1,0:T(8,128)(2,1)S(1)} fusion(bf16[1,1024,7168]{2,1,0:T(8,128)(2,1)} %param.25, bf16[16,7168]{1,0:T(8,128)(2,1)S(1)} %reshape.93, bf16[1,7168,1024]{2,1,0:T(8,128)(2,1)} %param.24, f32[16,1024]{1,0:T(8,128)S(1)} %fusion.21), kind=kOutput, calls=%fused_computation.27 | convolution fusion | flops 469975040 | bytes 29884416 | tf_op jit(solution)/shard_map/dot_general | solution.py:119
  50.2 0.8 %reshape.94 = bf16[8,2,7168]{2,1,0:T(2,128)(2,1)} reshape(bf16[16,7168]{1,0:T(8,128)(2,1)S(1)} %fusion.23) | data formatting | bytes 458752 | tf_op jit(solution)/shard_map/reshape | solution.py:122
  51.0 3.4 %all-to-all-start.1 = ((bf16[8,2,7168]{2,1,0:T(2,128)(2,1)}), bf16[8,2,7168]{2,1,0:T(2,128)(2,1)S(1)}, u32[]{:S(2)}, u32[]{:S(2)}) async-start(bf16[8,2,7168]{2,1,0:T(2,128)(2,1)} %reshape.94), calls=%async_computation.1 | async-start | bytes 458752 | tf_op jit(solution)/shard_map/all_to_all | solution.py:123
  54.4 0.2 fusion.36
  54.6 0.1 divide_convert_fusion
  54.7 0.1 fusion.44
  54.8 7.7 %all-to-all-done.1 = bf16[8,2,7168]{2,1,0:T(2,128)(2,1)S(1)} async-done(((bf16[8,2,7168]{2,1,0:T(2,128)(2,1)}), bf16[8,2,7168]{2,1,0:T(2,128)(2,1)S(1)}, u32[]{:S(2)}, u32[]{:S(2)}) %all-to-all-start.1) | async-done | bytes 229408 | tf_op jit(solution)/shard_map/all_to_all | solution.py:123
  62.5 0.2 convolution_bitcast_fusion.1
  62.7 0.1 constant_dynamic-slice_fusion.2
  62.8 0.1 collective-permute-start.3
  62.9 1.7 %collective-permute-start.5 = (f32[1,7168]{1,0:T(1,128)S(1)}, f32[1,7168]{1,0:T(1,128)S(1)}, u32[]{:S(2)}, u32[]{:S(2)}) collective-permute-start(f32[1,7168]{1,0:T(1,128)S(1)} %get-tuple-element.125), channel_id=1, source_target_pairs={{0,3},{1,0},{2,1},{3,2},{4,7},{5,4},{6,5},{7,6},{8,11},{9,8},{10,9... | collective-permute-start | bytes 86024 | tf_op jit(solution)/shard_map/ppermute | solution.py:135
  64.6 0.8 %collective-permute-start.4 = (f32[1,7168]{1,0:T(1,128)S(1)}, f32[1,7168]{1,0:T(1,128)S(1)}, u32[]{:S(2)}, u32[]{:S(2)}) collective-permute-start(f32[1,7168]{1,0:T(1,128)S(1)} %get-tuple-element.126), channel_id=1, source_target_pairs={{0,2},{1,3},{2,0},{3,1},{4,6},{5,7},{6,4},{7,5},{8,10},{9,11},{10,... | collective-permute-start | bytes 86024 | tf_op jit(solution)/shard_map/ppermute | solution.py:135
  65.5 0.0 copy-done
  65.5 0.2 while.21
  65.5 0.2 fusion.75
  65.7 0.7 convert_element_type.46
  66.4 0.0 collective-permute-done.3
  66.4 0.0 collective-permute-done.5
  66.4 2.1 %collective-permute-done.4 = f32[1,7168]{1,0:T(1,128)S(1)} collective-permute-done((f32[1,7168]{1,0:T(1,128)S(1)}, f32[1,7168]{1,0:T(1,128)S(1)}, u32[]{:S(2)}, u32[]{:S(2)}) %collective-permute-start.4) | collective-permute-done | bytes 28704 | tf_op jit(solution)/shard_map/ppermute | solution.py:135
  68.5 0.7 add_convert_fusion
  (8 shorter events, 0.1 us)
Async XLA Ops:
  2.2 3.9 %collective-permute-start = (bf16[1,7184]{1,0:T(2,128)(2,1)S(1)}, bf16[1,7184]{1,0:T(2,128)(2,1)S(1)}, u32[]{:S(2)}, u32[]{:S(2)}) collective-permute-start(bf16[1,7184]{1,0:T(2,128)(2,1)S(1)} %concatenate.9), channel_id=1, source_target_pairs={{0,1},{1,2},{2,3},{3,0},{4,5},{5,6},{6,7},{7,4},{8,9},{9,10},{10,1... | collective-permute-start | bytes 43112 | tf_op jit(solution)/shard_map/ppermute | solution.py:83
  6.1 3.3 %collective-permute-start.1 = (bf16[1,7184]{1,0:T(2,128)(2,1)S(1)}, bf16[1,7184]{1,0:T(2,128)(2,1)S(1)}, u32[]{:S(2)}, u32[]{:S(2)}) collective-permute-start(bf16[1,7184]{1,0:T(2,128)(2,1)S(1)} %collective-permute-done), channel_id=1, source_target_pairs={{0,1},{1,2},{2,3},{3,0},{4,5},{5,6},{6,7},{7,4},{8,9},{9,10},{10,1... | collective-permute-start | bytes 43112 | tf_op jit(solution)/shard_map/ppermute | solution.py:83
  9.4 3.3 %collective-permute-start.2 = (bf16[1,7184]{1,0:T(2,128)(2,1)S(1)}, bf16[1,7184]{1,0:T(2,128)(2,1)S(1)}, u32[]{:S(2)}, u32[]{:S(2)}) collective-permute-start(bf16[1,7184]{1,0:T(2,128)(2,1)S(1)} %collective-permute-done.1), channel_id=1, source_target_pairs={{0,1},{1,2},{2,3},{3,0},{4,5},{5,6},{6,7},{7,4},{8,9},{9,10},{10,1... | collective-permute-start | bytes 43112 | tf_op jit(solution)/shard_map/ppermute | solution.py:83
  14.5 15.2 %all-to-all-start = ((bf16[8,2,7168]{2,1,0:T(2,128)(2,1)}), bf16[8,2,7168]{2,1,0:T(2,128)(2,1)S(1)}, u32[]{:S(2)}, u32[]{:S(2)}) async-start(bf16[8,2,7168]{2,1,0:T(2,128)(2,1)} %copy.26), calls=%async_computation | async-start | bytes 458752 | tf_op jit(solution)/shard_map/all_to_all | solution.py:113
  36.9 28.6 %copy-start = (bf16[1,256,512]{2,1,0:T(8,128)(2,1)S(1)}, bf16[1,256,512]{2,1,0:T(8,128)(2,1)}, u32[]{:S(2)}) copy-start(bf16[1,256,512]{2,1,0:T(8,128)(2,1)} %get-tuple-element.263) | copy-start | bytes 786436
  51.0 11.5 %all-to-all-start.1 = ((bf16[8,2,7168]{2,1,0:T(2,128)(2,1)}), bf16[8,2,7168]{2,1,0:T(2,128)(2,1)S(1)}, u32[]{:S(2)}, u32[]{:S(2)}) async-start(bf16[8,2,7168]{2,1,0:T(2,128)(2,1)} %reshape.94), calls=%async_computation.1 | async-start | bytes 458752 | tf_op jit(solution)/shard_map/all_to_all | solution.py:123
  62.8 3.6 %collective-permute-start.3 = (f32[1,7168]{1,0:T(1,128)S(1)}, f32[1,7168]{1,0:T(1,128)S(1)}, u32[]{:S(2)}, u32[]{:S(2)}) collective-permute-start(f32[1,7168]{1,0:T(1,128)S(1)} %get-tuple-element.124), channel_id=1, source_target_pairs={{0,1},{1,2},{2,3},{3,0},{4,5},{5,6},{6,7},{7,4},{8,9},{9,10},{10,1... | collective-permute-start | bytes 86024 | tf_op jit(solution)/shard_map/ppermute | solution.py:135
  62.9 3.5 %collective-permute-start.5 = (f32[1,7168]{1,0:T(1,128)S(1)}, f32[1,7168]{1,0:T(1,128)S(1)}, u32[]{:S(2)}, u32[]{:S(2)}) collective-permute-start(f32[1,7168]{1,0:T(1,128)S(1)} %get-tuple-element.125), channel_id=1, source_target_pairs={{0,3},{1,0},{2,1},{3,2},{4,7},{5,4},{6,5},{7,6},{8,11},{9,8},{10,9... | collective-permute-start | bytes 86024 | tf_op jit(solution)/shard_map/ppermute | solution.py:135
  64.6 3.9 %collective-permute-start.4 = (f32[1,7168]{1,0:T(1,128)S(1)}, f32[1,7168]{1,0:T(1,128)S(1)}, u32[]{:S(2)}, u32[]{:S(2)}) collective-permute-start(f32[1,7168]{1,0:T(1,128)S(1)} %get-tuple-element.126), channel_id=1, source_target_pairs={{0,2},{1,3},{2,0},{3,1},{4,6},{5,7},{6,4},{7,5},{8,10},{9,11},{10,... | collective-permute-start | bytes 86024 | tf_op jit(solution)/shard_map/ppermute | solution.py:135
